TPU v7x, 128 devices: a whole 4x4x4 slice. The times are simulated.
128 devices in a mesh: dom: 8 (over x, z_hi), grid: 16 (over z_lo, y, core).
Axes of the slice: x: 4, y: 4, z: 4 (z_hi: 2, z_lo: 2; z = z_hi * 2 + z_lo), core: 2. Of those that a mesh axis runs over, the one named last changes fastest.
Arguments:
- bands: float32 [8, 4, 64, 48, 1280], P('dom', None, None, 'grid'), may hold values from -6 to 6
- potential: float32 [4, 48, 32, 256], P(None, 'grid', 'dom'), may hold values from -1 to 1
- domain_blocks: int32 [8, 6], replicated, may hold values from 0 to 31, as said below
- block_slots: int32 [32], replicated, may hold values from 0 to 31, as said below
- domain_offsets: int32 [8], replicated, may hold values from 0 to 3
Outputs:
- filtered: float32 [8, 4, 64, 48, 1280], P('dom', None, None, 'grid')
Inputs may be any that keep to these rules, and one draw needn't show every extreme that they name: `domain_blocks`: each row is 6 cyclically consecutive logical blocks. `block_slots`: a permutation; slot // 4 is the index of dom that stores the block; no domain has more than 1 of its blocks stored on one index of dom, and some domain has exactly 1.
All inputs are finite; a program needn't handle non-finite values.
Results may differ from a plain program's by a relative error of at most 0.0003.
Values sent between devices are 32-bit elements; how exact they have to be, the bound alone decides.
No kernel may reach another device: no remote copies, remote signals or barrier semaphores. Data moves between devices by JAX's collectives and lax.ppermute only.
A program may use at most 128 MiB of HBM per device.

v0:
```python
import jax
import jax.numpy as jnp
from jax import lax
from jax.sharding import PartitionSpec as P

DZ = 64
OVL = 6
CELLS = 1280
e_half = 4.5
centre = 5.0
sigma_one = e_half / (-3.5 - centre)
sigma_two = 1.0 / (2.0 / sigma_one - sigma_one)
sigma_three = 1.0 / (2.0 / sigma_one - sigma_two)
rashba = 0.3


def extended(block, sides, width):
    for axis, dim in sides:
        count = lax.axis_size(axis)
        forward = [(i, i + 1) for i in range(count - 1)]
        backward = [(target, source) for source, target in forward]
        low = lax.ppermute(
            lax.slice_in_dim(block, block.shape[dim] - width, None, axis=dim), axis, forward
        )
        high = lax.ppermute(lax.slice_in_dim(block, 0, width, axis=dim), axis, backward)
        block = jnp.concatenate([low, block, high], axis=dim)
    return block


def along(field, steps):
    zeros = jnp.zeros(field.shape[:-1] + (abs(steps),), jnp.float32)
    if steps > 0:
        return jnp.concatenate([field[..., steps:], zeros], axis=-1)
    return jnp.concatenate([zeros, field[..., :steps]], axis=-1)


def apply_h(padded, fields):
    middle = padded[:, :, 1:-1]
    x_next = padded[:, :, 2:]
    x_prev = padded[:, :, :-2]
    cell_ids = jnp.arange(middle.shape[-1]) % DZ
    z_high = (cell_ids != DZ - 1).astype(jnp.float32)
    z_low = (cell_ids != 0).astype(jnp.float32)
    y_next = along(middle, DZ)
    y_prev = along(middle, -DZ)
    z_next = along(middle, 1) * z_high
    z_prev = along(middle, -1) * z_low
    lapl = x_next + x_prev + y_next + y_prev + z_next + z_prev - 6.0 * middle
    diff_x = 0.5 * (x_next - x_prev)
    diff_y = 0.5 * (y_next - y_prev)
    pot_v, mag_x, mag_y, mag_z = (
        fields[0][None],
        fields[1][None],
        fields[2][None],
        fields[3][None],
    )
    a_up, b_up, a_dn, b_dn = (middle[0], middle[1], middle[2], middle[3])
    out_a = (
        -0.5 * lapl[0]
        + pot_v * a_up
        + mag_z * a_up
        + mag_x * a_dn
        + mag_y * b_dn
        + rashba * (diff_y[3] + diff_x[2])
    )
    out_b = (
        -0.5 * lapl[1]
        + pot_v * b_up
        + mag_z * b_up
        + mag_x * b_dn
        - mag_y * a_dn
        + rashba * (diff_x[3] - diff_y[2])
    )
    out_c = (
        -0.5 * lapl[2]
        + pot_v * a_dn
        + mag_x * a_up
        - mag_y * b_up
        - mag_z * a_dn
        + rashba * (diff_y[1] - diff_x[0])
    )
    out_d = (
        -0.5 * lapl[3]
        + pot_v * b_dn
        + mag_x * b_up
        + mag_y * a_up
        - mag_z * b_dn
        - rashba * (diff_y[0] + diff_x[1])
    )
    return jnp.stack([out_a, out_b, out_c, out_d])


def neighbours(field):
    return extended(field, (("grid", 2),), 1)


def per_device(bands, potential, domain_blocks, block_slots, domain_offsets):
    spinors = bands[0]
    planes = spinors.shape[2]
    block_cells = potential.shape[3]
    domain = lax.axis_index("dom")
    slot_ids = block_slots[domain_blocks]
    gathered = lax.all_gather(potential, "dom", axis=2, tiled=True)
    picked = jnp.take(gathered, slot_ids[domain], axis=2)
    window = picked.reshape(4, planes, OVL * block_cells)
    first_cell = domain_offsets[domain] * DZ
    fields = lax.dynamic_slice_in_dim(window, first_cell, CELLS, 2)
    first = sigma_one / e_half * (apply_h(neighbours(spinors), fields) - centre * spinors)
    second = (
        2.0 * sigma_two / e_half * (apply_h(neighbours(first), fields) - centre * first)
        - sigma_one * sigma_two * spinors
    )
    third = (
        2.0 * sigma_three / e_half * (apply_h(neighbours(second), fields) - centre * second)
        - sigma_two * sigma_three * first
    )
    return third[None]


def solution(mesh):
    placed = (P("dom", None, None, "grid", None), P(None, "grid", "dom", None), P(), P(), P())
    return jax.shard_map(
        per_device,
        mesh=mesh,
        in_specs=placed,
        out_specs=P("dom", None, None, "grid", None),
        check_vma=False,
    )
```

profile of v0, /device:TPU:25, one launch (start us, length us, event | category | flops | bytes accessed | tf_op | source)
XLA Modules:
  0.0 171.0 jit_solution(2017998420111669350)
XLA Ops:
  0.0 2.0 %fusion.99 = (f32[4,64,1,1280]{3,1,2,0:T(8,128)S(1)}, f32[4,64,1,1280]{3,1,2,0:T(8,128)S(1)}) fusion(f32[4,64,3,1280]{3,1,2,0:T(8,128)} %bitcast.95), kind=kLoop, calls=%fused_computation.176 | loop fusion | bytes 5242880 | tf_op jit(solution)/shard_map/slice | solution.py:23
  2.0 3.8 %collective-permute-start.1 = (f32[4,64,1,1280]{3,1,2,0:T(8,128)S(1)}, f32[4,64,1,1280]{3,1,2,0:T(8,128)}, u32[]{:S(2)}, u32[]{:S(2)}) collective-permute-start(f32[4,64,1,1280]{3,1,2,0:T(8,128)S(1)} %get-tuple-element.41), channel_id=1, source_target_pairs={{0,1},{1,2},{2,3},{3,4},{4,5},{5,6},{6,7},{7,8},{8,9},{9,10},{10,1... | collective-permute-start | bytes 3932168 | tf_op jit(solution)/shard_map/ppermute | solution.py:22
  5.8 1.9 %collective-permute-start = (f32[4,64,1,1280]{3,1,2,0:T(8,128)S(1)}, f32[4,64,1,1280]{3,1,2,0:T(8,128)}, u32[]{:S(2)}, u32[]{:S(2)}) collective-permute-start(f32[4,64,1,1280]{3,1,2,0:T(8,128)S(1)} %get-tuple-element.42), channel_id=1, source_target_pairs={{1,0},{2,1},{3,2},{4,3},{5,4},{6,5},{7,6},{8,7},{9,8},{10,9},{11,1... | collective-permute-start | bytes 3932168 | tf_op jit(solution)/shard_map/ppermute | solution.py:25
  8.8 7.6 %fusion.97 = (f32[4,64,3,1279]{3,1,2,0:T(8,128)}, f32[4,64,3,1279]{3,1,2,0:T(8,128)}) fusion(f32[4,64,3,1280]{3,1,2,0:T(8,128)} %bitcast.96), kind=kLoop, calls=%fused_computation.174 | loop fusion | bytes 15716352 | tf_op jit(solution)/shard_map/slice | solution.py:33
  17.8 28.8 %all_gather.3 = f32[4,3,32,256]{3,0,2,1:T(4,128)S(1)} all-gather(f32[4,3,4,256]{3,0,2,1:T(4,128)S(1)} %copy.6), channel_id=1, replica_groups=mesh['dom'=8,'grid'=16] {'dom'}, dimensions={2}, use_global_device_ids=true | all-gather | bytes 442368 | tf_op jit(solution)/shard_map/all_gather | solution.py:103
  47.5 7.7 %fusion.98 = (f32[4,64,3,1216]{3,1,2,0:T(8,128)}, f32[4,64,3,1216]{3,1,2,0:T(8,128)}) fusion(f32[4,64,3,1280]{3,1,2,0:T(8,128)} %bitcast.97), kind=kLoop, calls=%fused_computation.175 | loop fusion | bytes 14942208 | tf_op jit(solution)/shard_map/slice | solution.py:33
  55.3 8.5 %multiply_subtract_fusion.2 = (f32[4,64,3,1280]{3,1,2,0:T(8,128)S(1)}, f32[4,64,3,1280]{3,1,2,0:T(8,128)}, f32[4,64,3,1280]{3,1,2,0:T(8,128)}) fusion(f32[4,64,3,1280]{3,1,2,0:T(8,128)S(1)} %bitcast.98, f32[4,64,3,1279]{3,1,2,0:T(8,128)} %get-tuple-element.38, f32[4,64,3,1279]{3,1,2,0:T(8,128)S(1)} %copy-done.11, f32[4,64,3,1216]{3,1,2,0:T(8,128)} %get-tuple-element.40, ...), kind=kLoop, calls=%fused_computation.28 | loop fusion | flops 14745600 | bytes 33689600 | tf_op jit(solution)/shard_map/sub | solution.py:48
  63.8 3.5 %fusion.72 = (f32[1,64,3,1280]{3,1,2,0:T(8,128)S(1)}, f32[1,64,3,1280]{3,1,2,0:T(8,128)S(1)}) fusion(f32[4,64,3,1280]{3,1,2,0:T(8,128)} %get-tuple-element.22, f32[4,64,3,1280]{3,1,2,0:T(8,128)} %get-tuple-element.24, f32[4,64,3,1280]{3,1,2,0:T(8,128)S(1)} %get-tuple-element.21, f32[1,4,64,3,1280]{4,2,3,1,0:T(8,128)S(1)} %copy-done.2, ...), kind=kLoop, calls=%fused_computation.116 | loop fusion | flops 5898240 | bytes 11857920 | tf_op jit(solution)/shard_map/add | solution.py:67
  68.3 1.1 fusion.78
  70.1 11.8 %collective-permute-start.3 = (f32[4,64,1,1280]{3,1,2,0:T(8,128)S(1)}, f32[4,64,1,1280]{3,1,2,0:T(8,128)S(1)}, u32[]{:S(2)}, u32[]{:S(2)}) collective-permute-start(f32[4,64,1,1280]{3,1,2,0:T(8,128)S(1)} %get-tuple-element.35), channel_id=1, source_target_pairs={{0,1},{1,2},{2,3},{3,4},{4,5},{5,6},{6,7},{7,8},{8,9},{9,10},{10,1... | collective-permute-start | bytes 3932168 | tf_op jit(solution)/shard_map/ppermute | solution.py:22
  82.0 2.1 %collective-permute-start.2 = (f32[4,64,1,1280]{3,1,2,0:T(8,128)S(1)}, f32[4,64,1,1280]{3,1,2,0:T(8,128)S(1)}, u32[]{:S(2)}, u32[]{:S(2)}) collective-permute-start(f32[4,64,1,1280]{3,1,2,0:T(8,128)S(1)} %get-tuple-element.36), channel_id=1, source_target_pairs={{1,0},{2,1},{3,2},{4,3},{5,4},{6,5},{7,6},{8,7},{9,8},{10,9},{11,1... | collective-permute-start | bytes 3932168 | tf_op jit(solution)/shard_map/ppermute | solution.py:25
  84.1 4.4 %fusion.94 = (f32[4,64,3,1279]{3,1,2,0:T(8,128)}, f32[4,64,3,1279]{3,1,2,0:T(8,128)}) fusion(f32[4,64,3,1280]{3,1,2,0:T(8,128)S(1)} %broadcast_multiply_fusion), kind=kLoop, calls=%fused_computation.171 | loop fusion | bytes 15716352 | tf_op jit(solution)/shard_map/slice | solution.py:33
  88.5 4.4 %fusion.95 = (f32[4,64,3,1216]{3,1,2,0:T(8,128)}, f32[4,64,3,1216]{3,1,2,0:T(8,128)}) fusion(f32[4,64,3,1280]{3,1,2,0:T(8,128)S(1)} %broadcast_multiply_fusion), kind=kLoop, calls=%fused_computation.172 | loop fusion | bytes 14942208 | tf_op jit(solution)/shard_map/slice | solution.py:33
  93.0 3.6 %collective-permute-done.3 = f32[4,64,1,1280]{3,1,2,0:T(8,128)S(1)} collective-permute-done((f32[4,64,1,1280]{3,1,2,0:T(8,128)S(1)}, f32[4,64,1,1280]{3,1,2,0:T(8,128)S(1)}, u32[]{:S(2)}, u32[]{:S(2)}) %collective-permute-start.3) | collective-permute-done | bytes 1310752 | tf_op jit(solution)/shard_map/ppermute | solution.py:22
  96.5 6.5 %collective-permute-done.2 = f32[4,64,1,1280]{3,1,2,0:T(8,128)S(1)} collective-permute-done((f32[4,64,1,1280]{3,1,2,0:T(8,128)S(1)}, f32[4,64,1,1280]{3,1,2,0:T(8,128)S(1)}, u32[]{:S(2)}, u32[]{:S(2)}) %collective-permute-start.2) | collective-permute-done | bytes 1310752 | tf_op jit(solution)/shard_map/ppermute | solution.py:25
  103.0 2.5 %subtract_multiply_fusion.2 = f32[4,64,3,1280]{3,1,2,0:T(8,128)} fusion(f32[4,64,1,1280]{3,1,2,0:T(8,128)S(1)} %collective-permute-done.2, f32[4,64,3,1280]{3,1,2,0:T(8,128)S(1)} %broadcast_multiply_fusion, f32[4,64,1,1280]{3,1,2,0:T(8,128)S(1)} %collective-permute-done.3), kind=kLoop, calls=%fused_computation.23 | loop fusion | flops 3932160 | bytes 10485760 | tf_op jit(solution)/shard_map/mul | solution.py:49
  105.5 9.3 %multiply_subtract_fusion.1 = (f32[4,64,3,1280]{3,1,2,0:T(8,128)}, f32[4,64,3,1280]{3,1,2,0:T(8,128)}) fusion(f32[4,64,3,1279]{3,1,2,0:T(8,128)} %get-tuple-element.32, f32[4,64,3,1279]{3,1,2,0:T(8,128)} %get-tuple-element.31, f32[4,64,3,1216]{3,1,2,0:T(8,128)} %get-tuple-element.34, f32[4,64,3,1216]{3,1,2,0:T(8,128)} %get-tuple-element.33, ...), kind=kLoop, calls=%fused_computation.25 | loop fusion | flops 17694720 | bytes 37621760 | tf_op jit(solution)/shard_map/sub | solution.py:48
  114.8 4.1 %fusion.48 = (f32[1,64,3,1280]{3,1,2,0:T(8,128)S(1)}, f32[1,64,3,1280]{3,1,2,0:T(8,128)S(1)}) fusion(f32[4,64,3,1280]{3,1,2,0:T(8,128)} %get-tuple-element.20, f32[4,64,3,1280]{3,1,2,0:T(8,128)} %subtract_multiply_fusion.2, f32[4,64,3,1280]{3,1,2,0:T(8,128)} %get-tuple-element.19, f32[4,64,3,1280]{3,1,2,0:T(8,128)S(1)} %broadcast_multiply_fusion, ...), kind=kLoop, calls=%fused_computation.84 | loop fusion | flops 5898240 | bytes 11857920 | tf_op jit(solution)/shard_map/add | solution.py:67
  119.9 1.1 copy-done.5
  122.0 1.1 fusion.1
  123.5 1.9 %collective-permute-start.5 = (f32[4,64,1,1280]{3,1,2,0:T(8,128)S(1)}, f32[4,64,1,1280]{3,1,2,0:T(8,128)S(1)}, u32[]{:S(2)}, u32[]{:S(2)}) collective-permute-start(f32[4,64,1,1280]{3,1,2,0:T(8,128)S(1)} %get-tuple-element.29), channel_id=1, source_target_pairs={{0,1},{1,2},{2,3},{3,4},{4,5},{5,6},{6,7},{7,8},{8,9},{9,10},{10,1... | collective-permute-start | bytes 3932168 | tf_op jit(solution)/shard_map/ppermute | solution.py:22
  125.4 2.6 %collective-permute-start.4 = (f32[4,64,1,1280]{3,1,2,0:T(8,128)S(1)}, f32[4,64,1,1280]{3,1,2,0:T(8,128)S(1)}, u32[]{:S(2)}, u32[]{:S(2)}) collective-permute-start(f32[4,64,1,1280]{3,1,2,0:T(8,128)S(1)} %get-tuple-element.30), channel_id=1, source_target_pairs={{1,0},{2,1},{3,2},{4,3},{5,4},{6,5},{7,6},{8,7},{9,8},{10,9},{11,1... | collective-permute-start | bytes 3932168 | tf_op jit(solution)/shard_map/ppermute | solution.py:25
  128.0 4.5 %fusion.92 = (f32[4,64,3,1216]{3,1,2,0:T(8,128)}, f32[4,64,3,1216]{3,1,2,0:T(8,128)}) fusion(f32[4,64,3,1280]{3,1,2,0:T(8,128)S(1)} %fusion.1), kind=kLoop, calls=%fused_computation.169 | loop fusion | bytes 14942208 | tf_op jit(solution)/shard_map/slice | solution.py:33
  132.5 4.5 %fusion.91 = (f32[4,64,3,1279]{3,1,2,0:T(8,128)}, f32[4,64,3,1279]{3,1,2,0:T(8,128)}) fusion(f32[4,64,3,1280]{3,1,2,0:T(8,128)S(1)} %fusion.1), kind=kLoop, calls=%fused_computation.168 | loop fusion | bytes 15716352 | tf_op jit(solution)/shard_map/slice | solution.py:33
  137.1 2.9 %collective-permute-done.5 = f32[4,64,1,1280]{3,1,2,0:T(8,128)S(1)} collective-permute-done((f32[4,64,1,1280]{3,1,2,0:T(8,128)S(1)}, f32[4,64,1,1280]{3,1,2,0:T(8,128)S(1)}, u32[]{:S(2)}, u32[]{:S(2)}) %collective-permute-start.5) | collective-permute-done | bytes 1310752 | tf_op jit(solution)/shard_map/ppermute | solution.py:22
  139.9 6.5 %collective-permute-done.4 = f32[4,64,1,1280]{3,1,2,0:T(8,128)S(1)} collective-permute-done((f32[4,64,1,1280]{3,1,2,0:T(8,128)S(1)}, f32[4,64,1,1280]{3,1,2,0:T(8,128)S(1)}, u32[]{:S(2)}, u32[]{:S(2)}) %collective-permute-start.4) | collective-permute-done | bytes 1310752 | tf_op jit(solution)/shard_map/ppermute | solution.py:25
  146.4 1.2 copy-done.17
  147.6 10.7 %multiply_subtract_fusion = (f32[4,64,3,1280]{3,1,2,0:T(8,128)}, f32[4,64,3,1280]{3,1,2,0:T(8,128)}, f32[4,64,3,1280]{3,1,2,0:T(8,128)}) fusion(f32[4,64,3,1280]{3,1,2,0:T(8,128)S(1)} %fusion.1, f32[4,64,3,1279]{3,1,2,0:T(8,128)} %get-tuple-element.26, f32[4,64,3,1279]{3,1,2,0:T(8,128)} %get-tuple-element.25, f32[4,64,3,1216]{3,1,2,0:T(8,128)} %get-tuple-element.28, ...), kind=kLoop, calls=%fused_computation.22 | loop fusion | flops 14745600 | bytes 33689600 | tf_op jit(solution)/shard_map/sub | solution.py:48
  158.4 4.1 %fusion.23 = (f32[1,1,64,3,1280]{4,2,3,1,0:T(8,128)S(1)}, f32[1,1,64,3,1280]{4,2,3,1,0:T(8,128)S(1)}) fusion(f32[4,64,3,1280]{3,1,2,0:T(8,128)} %get-tuple-element.18, f32[4,64,3,1280]{3,1,2,0:T(8,128)} %get-tuple-element.23, f32[4,64,3,1280]{3,1,2,0:T(8,128)} %get-tuple-element.17, f32[4,64,3,1280]{3,1,2,0:T(8,128)S(1)} %fusion.1, ...), kind=kLoop, calls=%fused_computation.51 | loop fusion | flops 5898240 | bytes 11857920 | tf_op jit(solution)/shard_map/stack | solution.py:90
  163.4 1.1 copy-done.8
  164.5 2.0 %fusion.30 = (f32[1,1,64,3,1280]{4,2,3,1,0:T(8,128)S(1)}, f32[1,1,64,3,1280]{4,2,3,1,0:T(8,128)}) fusion(f32[4,64,3,1280]{3,1,2,0:T(8,128)S(1)} %copy-done.8, f32[4,64,3,1280]{3,1,2,0:T(8,128)S(1)} %copy-done.7, f32[4,64,3,1280]{3,1,2,0:T(8,128)S(1)} %copy-done.6, f32[4,64,3,1280]{3,1,2,0:T(8,128)S(1)} %fusion.1, f32[3,1280]{1,0:T(4,128)S(1)} %get-tuple-element.49, ...), kind=kLoop, calls=%fused_computation.60 | loop fusion | flops 5898240 | bytes 11857920 | tf_op jit(solution)/shard_map/stack | solution.py:90
  166.5 4.5 %fusion.3 = f32[1,4,64,3,1280]{4,2,3,1,0:T(8,128)} fusion(f32[1,1,64,3,1280]{4,2,3,1,0:T(8,128)} %get-tuple-element.6, f32[1,1,64,3,1280]{4,2,3,1,0:T(8,128)S(1)} %get-tuple-element.8, f32[1,1,64,3,1280]{4,2,3,1,0:T(8,128)S(1)} %get-tuple-element.7, f32[1,1,64,3,1280]{4,2,3,1,0:T(8,128)S(1)} %get-tuple-element.5, f32[1,1,64,3,1280]{4,2,3,1,0:T(8,128)S(1)} %bitcast.106, ...), kind=kLoop, calls=%fused_computation.14 | loop fusion | flops 20643840 | bytes 19660800 | tf_op jit(solution)/shard_map/sub | solution.py:114
  (65 shorter events, 7.7 us)
Async XLA Ops:
  0.0 7.8 %copy-start = (s32[32]{0:T(128)S(1)}, s32[32]{0:T(128)}, u32[]{:S(2)}) copy-start(s32[32]{0:T(128)} %param.8) | copy-start | bytes 388
  0.0 7.7 %copy-start.19 = (s32[8,6]{1,0:T(8,128)S(1)}, s32[8,6]{1,0:T(8,128)}, u32[]{:S(2)}) copy-start(s32[8,6]{1,0:T(8,128)} %param.7) | copy-start | bytes 580
  2.0 53.3 %collective-permute-start.1 = (f32[4,64,1,1280]{3,1,2,0:T(8,128)S(1)}, f32[4,64,1,1280]{3,1,2,0:T(8,128)}, u32[]{:S(2)}, u32[]{:S(2)}) collective-permute-start(f32[4,64,1,1280]{3,1,2,0:T(8,128)S(1)} %get-tuple-element.41), channel_id=1, source_target_pairs={{0,1},{1,2},{2,3},{3,4},{4,5},{5,6},{6,7},{7,8},{8,9},{9,10},{10,1... | collective-permute-start | bytes 3932168 | tf_op jit(solution)/shard_map/ppermute | solution.py:22
  5.8 49.5 %collective-permute-start = (f32[4,64,1,1280]{3,1,2,0:T(8,128)S(1)}, f32[4,64,1,1280]{3,1,2,0:T(8,128)}, u32[]{:S(2)}, u32[]{:S(2)}) collective-permute-start(f32[4,64,1,1280]{3,1,2,0:T(8,128)S(1)} %get-tuple-element.42), channel_id=1, source_target_pairs={{1,0},{2,1},{3,2},{4,3},{5,4},{6,5},{7,6},{8,7},{9,8},{10,9},{11,1... | collective-permute-start | bytes 3932168 | tf_op jit(solution)/shard_map/ppermute | solution.py:25
  8.7 7.7 %copy-start.20 = (s32[8]{0:T(128)S(1)}, s32[8]{0:T(128)}, u32[]{:S(2)}) copy-start(s32[8]{0:T(128)} %param.9) | copy-start | bytes 100
  8.7 9.0 %copy-start.18 = (f32[4,3,4,256]{3,2,1,0:T(4,128)S(1)}, f32[4,3,4,256]{3,2,1,0:T(4,128)}, u32[]{:S(2)}) copy-start(f32[4,3,4,256]{3,2,1,0:T(4,128)} %param.6) | copy-start | bytes 147460
  47.5 7.8 %copy-start.2 = (f32[1,4,64,3,1280]{4,2,3,1,0:T(8,128)S(1)}, f32[1,4,64,3,1280]{4,2,3,1,0:T(8,128)}, u32[]{:S(2)}) copy-start(f32[1,4,64,3,1280]{4,2,3,1,0:T(8,128)} %param.5) | copy-start | bytes 11796484
  47.5 7.8 %copy-start.11 = (f32[4,64,3,1279]{3,1,2,0:T(8,128)S(1)}, f32[4,64,3,1279]{3,1,2,0:T(8,128)}, u32[]{:S(2)}) copy-start(f32[4,64,3,1279]{3,1,2,0:T(8,128)} %get-tuple-element.37) | copy-start | bytes 11787268
  63.8 3.5 %copy-start.9 = (f32[4,64,3,1280]{3,1,2,0:T(8,128)S(1)}, f32[4,64,3,1280]{3,1,2,0:T(8,128)}, u32[]{:S(2)}) copy-start(f32[4,64,3,1280]{3,1,2,0:T(8,128)} %get-tuple-element.22) | copy-start | bytes 11796484
  63.8 4.5 %copy-start.10 = (f32[4,64,3,1280]{3,1,2,0:T(8,128)S(1)}, f32[4,64,3,1280]{3,1,2,0:T(8,128)}, u32[]{:S(2)}) copy-start(f32[4,64,3,1280]{3,1,2,0:T(8,128)} %get-tuple-element.24) | copy-start | bytes 11796484
  70.1 26.4 %collective-permute-start.3 = (f32[4,64,1,1280]{3,1,2,0:T(8,128)S(1)}, f32[4,64,1,1280]{3,1,2,0:T(8,128)S(1)}, u32[]{:S(2)}, u32[]{:S(2)}) collective-permute-start(f32[4,64,1,1280]{3,1,2,0:T(8,128)S(1)} %get-tuple-element.35), channel_id=1, source_target_pairs={{0,1},{1,2},{2,3},{3,4},{4,5},{5,6},{6,7},{7,8},{8,9},{9,10},{10,1... | collective-permute-start | bytes 3932168 | tf_op jit(solution)/shard_map/ppermute | solution.py:22
  82.0 21.0 %collective-permute-start.2 = (f32[4,64,1,1280]{3,1,2,0:T(8,128)S(1)}, f32[4,64,1,1280]{3,1,2,0:T(8,128)S(1)}, u32[]{:S(2)}, u32[]{:S(2)}) collective-permute-start(f32[4,64,1,1280]{3,1,2,0:T(8,128)S(1)} %get-tuple-element.36), channel_id=1, source_target_pairs={{1,0},{2,1},{3,2},{4,3},{5,4},{6,5},{7,6},{8,7},{9,8},{10,9},{11,1... | collective-permute-start | bytes 3932168 | tf_op jit(solution)/shard_map/ppermute | solution.py:25
  114.8 4.1 %copy-start.3 = (f32[4,64,3,1280]{3,1,2,0:T(8,128)S(1)}, f32[4,64,3,1280]{3,1,2,0:T(8,128)}, u32[]{:S(2)}) copy-start(f32[4,64,3,1280]{3,1,2,0:T(8,128)} %subtract_multiply_fusion.2) | copy-start | bytes 11796484
  114.8 5.1 %copy-start.4 = (f32[4,64,3,1280]{3,1,2,0:T(8,128)S(1)}, f32[4,64,3,1280]{3,1,2,0:T(8,128)}, u32[]{:S(2)}) copy-start(f32[4,64,3,1280]{3,1,2,0:T(8,128)} %get-tuple-element.19) | copy-start | bytes 11796484
  114.8 6.2 %copy-start.5 = (f32[4,64,3,1280]{3,1,2,0:T(8,128)S(1)}, f32[4,64,3,1280]{3,1,2,0:T(8,128)}, u32[]{:S(2)}) copy-start(f32[4,64,3,1280]{3,1,2,0:T(8,128)} %get-tuple-element.20) | copy-start | bytes 11796484
  122.0 1.2 copy-start.12
  122.0 1.2 copy-start.14
  123.5 16.5 %collective-permute-start.5 = (f32[4,64,1,1280]{3,1,2,0:T(8,128)S(1)}, f32[4,64,1,1280]{3,1,2,0:T(8,128)S(1)}, u32[]{:S(2)}, u32[]{:S(2)}) collective-permute-start(f32[4,64,1,1280]{3,1,2,0:T(8,128)S(1)} %get-tuple-element.29), channel_id=1, source_target_pairs={{0,1},{1,2},{2,3},{3,4},{4,5},{5,6},{6,7},{7,8},{8,9},{9,10},{10,1... | collective-permute-start | bytes 3932168 | tf_op jit(solution)/shard_map/ppermute | solution.py:22
  125.4 21.0 %collective-permute-start.4 = (f32[4,64,1,1280]{3,1,2,0:T(8,128)S(1)}, f32[4,64,1,1280]{3,1,2,0:T(8,128)S(1)}, u32[]{:S(2)}, u32[]{:S(2)}) collective-permute-start(f32[4,64,1,1280]{3,1,2,0:T(8,128)S(1)} %get-tuple-element.30), channel_id=1, source_target_pairs={{1,0},{2,1},{3,2},{4,3},{5,4},{6,5},{7,6},{8,7},{9,8},{10,9},{11,1... | collective-permute-start | bytes 3932168 | tf_op jit(solution)/shard_map/ppermute | solution.py:25
  139.9 6.5 %copy-start.16 = (f32[4,64,1,1280]{3,1,2,0:T(8,128)}, f32[4,64,1,1280]{3,1,2,0:T(8,128)S(1)}, u32[]{:S(2)}) copy-start(f32[4,64,1,1280]{3,1,2,0:T(8,128)S(1)} %collective-permute-done.5) | copy-start | bytes 3932164
  146.4 1.2 copy-start.17
  158.3 4.1 %copy-start.6 = (f32[4,64,3,1280]{3,1,2,0:T(8,128)S(1)}, f32[4,64,3,1280]{3,1,2,0:T(8,128)}, u32[]{:S(2)}) copy-start(f32[4,64,3,1280]{3,1,2,0:T(8,128)} %get-tuple-element.17) | copy-start | bytes 11796484
  158.3 5.1 %copy-start.7 = (f32[4,64,3,1280]{3,1,2,0:T(8,128)S(1)}, f32[4,64,3,1280]{3,1,2,0:T(8,128)}, u32[]{:S(2)}) copy-start(f32[4,64,3,1280]{3,1,2,0:T(8,128)} %get-tuple-element.18) | copy-start | bytes 11796484
  158.3 6.2 %copy-start.8 = (f32[4,64,3,1280]{3,1,2,0:T(8,128)S(1)}, f32[4,64,3,1280]{3,1,2,0:T(8,128)}, u32[]{:S(2)}) copy-start(f32[4,64,3,1280]{3,1,2,0:T(8,128)} %get-tuple-element.23) | copy-start | bytes 11796484
  164.5 2.0 %copy-start.13 = (f32[1,64,3,1280]{3,1,2,0:T(8,128)S(1)}, f32[1,64,3,1280]{3,1,2,0:T(8,128)}, u32[]{:S(2)}) copy-start(f32[1,64,3,1280]{3,1,2,0:T(8,128)} %copy-done.12) | copy-start | bytes 2949124
  164.5 2.0 %copy-start.15 = (f32[1,64,3,1280]{3,1,2,0:T(8,128)S(1)}, f32[1,64,3,1280]{3,1,2,0:T(8,128)}, u32[]{:S(2)}) copy-start(f32[1,64,3,1280]{3,1,2,0:T(8,128)} %copy-done.14) | copy-start | bytes 2949124
  166.5 4.5 %copy-start.1 = (s32[32]{0:T(128)S(1)}, s32[32]{0:T(128)}, u32[]{:S(2)}) copy-start(s32[32]{0:T(128)} %param.8) | copy-start | bytes 388
where the time goes:
time: 171 us
  other arithmetic  53 us (31%)
  local copies, waits for them, and re-layouts  44.6 us (26%)
  blocking collectives  28.8 us (17%)
  starting transfers between devices  24.2 us (14%)
  waiting for transfers between devices  19.4 us (11%)
    slice x6, local copies, waits for them, and re-layouts, along(): return jnp.concatenate([field[..., steps:], zeros], axis=-1)  33.3 us
    all_gather x1, blocking collectives, per_device(): gathered = lax.all_gather(potential, 'dom', axis=2, tiled=True)  28.8 us
    sub x3, other arithmetic, apply_h(): lapl = x_next + x_prev + y_next + y_prev + z_next + z_prev - 6.0 * middle  28.5 us
    ppermute x3, starting transfers between devices, extended(): lax.ppermute(lax.slice_in_dim(block, block.shape[dim] - width, None, axis...  17.5 us
    ppermute x3, waiting for transfers between devices, extended(): lax.ppermute(lax.slice_in_dim(block, 0, width, axis=dim), axis, backward)  13 us
    add x2, other arithmetic, apply_h(): -0.5 * lapl[1] + pot_v * b_up + mag_z * b_up + mag_x * b_dn - mag_y * a_dn  7.52 us
    ppermute x3, starting transfers between devices, extended(): lax.ppermute(lax.slice_in_dim(block, 0, width, axis=dim), axis, backward)  6.65 us
    unnamed x45, local copies, waits for them, and re-layouts  6.56 us
  transfers between devices with their start and end apart: 6, of which 4 were waited for; matrix products, arithmetic and copies ran while one was open for 21% of the time, Pallas kernels for 0%

commit v1 on v0

--- a/solution.py
+++ b/solution.py
@@ -100,7 +100,13 @@
     block_cells = potential.shape[3]
     domain = lax.axis_index("dom")
     slot_ids = block_slots[domain_blocks]
-    gathered = lax.all_gather(potential, "dom", axis=2, tiled=True)
+    lay_positions_all = lambda values, ax_name: jnp.concatenate(
+        lax.all_to_all(
+            jnp.stack([values for _ in range(lax.axis_size(ax_name))], axis=0), ax_name, 0, 0
+        ),
+        axis=2,
+    )
+    gathered = lay_positions_all(potential, "dom")
     picked = jnp.take(gathered, slot_ids[domain], axis=2)
     window = picked.reshape(4, planes, OVL * block_cells)
     first_cell = domain_offsets[domain] * DZ

time: 171 us -> 147 us (0.86)
  blocking collectives: 28.8 us -> 0 us
  waiting for transfers between devices: 19.4 us -> 25.9 us
  other arithmetic: 53 us -> 58 us
  local copies, waits for them, and re-layouts: 44.6 us -> 40 us
  starting transfers between devices: 24.2 us -> 21.5 us
    all_gather x1 -> x0, blocking collectives: 28.8 us -> none  [per_device(): gathered = lax.all_gather(potential, 'dom', axis=2, tiled=True)]
    ppermute x3, starting transfers between devices: 17.5 us -> 6.99 us  [extended(): lax.ppermute(lax.slice_in_dim(block, block.shape[dim] - width, None, axis...]
    all_to_all x0 -> x1, starting transfers between devices: none -> 7.33 us  [per_device(): lax.all_to_all(jnp.stack([values for _ in range(lax.axis_size(ax_name))],...]
    ppermute x3, waiting for transfers between devices: 13 us -> 19.6 us  [extended(): lax.ppermute(lax.slice_in_dim(block, 0, width, axis=dim), axis, backward)]
    slice x6, local copies, waits for them, and re-layouts: 33.3 us -> 26.9 us  [along(): return jnp.concatenate([field[..., steps:], zeros], axis=-1)]
    sub x3, other arithmetic: 28.5 us -> 33.5 us  [apply_h(): lapl = x_next + x_prev + y_next + y_prev + z_next + z_prev - 6.0 * middle]
    unnamed x45 -> x43, local copies, waits for them, and re-layouts: 6.56 us -> 7.36 us
  transfers between devices with their start and end apart: 6 -> 7, of which waited for: 4 -> 6; matrix products, arithmetic and copies ran while one was open for 21% -> 22% of each run, Pallas kernels for 0% -> 0%
where the time goes in v1:
time: 147 us; the launch traced here: 146 us
  other arithmetic  58 us (39%)
  local copies, waits for them, and re-layouts  40 us (27%)
  waiting for transfers between devices  25.9 us (18%)
  starting transfers between devices  21.5 us (15%)
    sub x3, other arithmetic, apply_h(): lapl = x_next + x_prev + y_next + y_prev + z_next + z_prev - 6.0 * middle  33.5 us
    slice x6, local copies, waits for them, and re-layouts, along(): return jnp.concatenate([field[..., steps:], zeros], axis=-1)  26.9 us
    ppermute x3, waiting for transfers between devices, extended(): lax.ppermute(lax.slice_in_dim(block, 0, width, axis=dim), axis, backward)  19.6 us
    add x2, other arithmetic, apply_h(): -0.5 * lapl[1] + pot_v * b_up + mag_z * b_up + mag_x * b_dn - mag_y * a_dn  7.52 us
    unnamed x43, local copies, waits for them, and re-layouts  7.36 us
    all_to_all x1, starting transfers between devices, per_device(): lax.all_to_all(jnp.stack([values for _ in range(lax.axis_size(ax_name))],...  7.33 us
    ppermute x3, starting transfers between devices, extended(): lax.ppermute(lax.slice_in_dim(block, 0, width, axis=dim), axis, backward)  7.14 us
    ppermute x3, starting transfers between devices, extended(): lax.ppermute(lax.slice_in_dim(block, block.shape[dim] - width, None, axis...  6.99 us
  transfers between devices with their start and end apart: 7, of which 6 were waited for; matrix products, arithmetic and copies ran while one was open for 22% of the time, Pallas kernels for 0%

profile of v1, /device:TPU:25, one launch (start us, length us, event | category | flops | bytes accessed | tf_op | source)
XLA Modules:
  0.0 146.3 jit_solution(8319654521154861921)
XLA Ops:
  1.7 7.3 %all-to-all-start = ((f32[8,4,3,4,256]{4,1,3,2,0:T(4,128)}), f32[8,4,3,4,256]{4,1,3,2,0:T(4,128)S(1)}, u32[]{:S(2)}, u32[]{:S(2)}) async-start(f32[8,4,3,4,256]{4,1,3,2,0:T(4,128)} %stack.60), calls=%async_computation | async-start | bytes 786432 | tf_op jit(solution)/shard_map/all_to_all | solution.py:104
  9.0 2.1 %fusion.99 = (f32[4,64,1,1280]{3,1,2,0:T(8,128)S(1)}, f32[4,64,1,1280]{3,1,2,0:T(8,128)S(1)}) fusion(f32[4,64,3,1280]{3,1,2,0:T(8,128)} %bitcast.97), kind=kLoop, calls=%fused_computation.176 | loop fusion | bytes 5242880 | tf_op jit(solution)/shard_map/slice | solution.py:23
  11.1 3.1 %collective-permute-start.1 = (f32[4,64,1,1280]{3,1,2,0:T(8,128)S(1)}, f32[4,64,1,1280]{3,1,2,0:T(8,128)}, u32[]{:S(2)}, u32[]{:S(2)}) collective-permute-start(f32[4,64,1,1280]{3,1,2,0:T(8,128)S(1)} %get-tuple-element.41), channel_id=1, source_target_pairs={{0,1},{1,2},{2,3},{3,4},{4,5},{5,6},{6,7},{7,8},{8,9},{9,10},{10,1... | collective-permute-start | bytes 3932168 | tf_op jit(solution)/shard_map/ppermute | solution.py:22
  14.3 1.9 %collective-permute-start = (f32[4,64,1,1280]{3,1,2,0:T(8,128)S(1)}, f32[4,64,1,1280]{3,1,2,0:T(8,128)}, u32[]{:S(2)}, u32[]{:S(2)}) collective-permute-start(f32[4,64,1,1280]{3,1,2,0:T(8,128)S(1)} %get-tuple-element.42), channel_id=1, source_target_pairs={{1,0},{2,1},{3,2},{4,3},{5,4},{6,5},{7,6},{8,7},{9,8},{10,9},{11,1... | collective-permute-start | bytes 3932168 | tf_op jit(solution)/shard_map/ppermute | solution.py:25
  16.2 4.5 %fusion.97 = (f32[4,64,3,1279]{3,1,2,0:T(8,128)}, f32[4,64,3,1279]{3,1,2,0:T(8,128)}) fusion(f32[4,64,3,1280]{3,1,2,0:T(8,128)S(1)} %bitcast.99), kind=kLoop, calls=%fused_computation.174 | loop fusion | bytes 15716352 | tf_op jit(solution)/shard_map/slice | solution.py:33
  20.8 4.5 %fusion.98 = (f32[4,64,3,1216]{3,1,2,0:T(8,128)}, f32[4,64,3,1216]{3,1,2,0:T(8,128)}) fusion(f32[4,64,3,1280]{3,1,2,0:T(8,128)S(1)} %bitcast.100), kind=kLoop, calls=%fused_computation.175 | loop fusion | bytes 14942208 | tf_op jit(solution)/shard_map/slice | solution.py:33
  28.8 6.6 %collective-permute-done = f32[4,64,1,1280]{3,1,2,0:T(8,128)} collective-permute-done((f32[4,64,1,1280]{3,1,2,0:T(8,128)S(1)}, f32[4,64,1,1280]{3,1,2,0:T(8,128)}, u32[]{:S(2)}, u32[]{:S(2)}) %collective-permute-start) | collective-permute-done | bytes 1310752 | tf_op jit(solution)/shard_map/ppermute | solution.py:25
  35.4 13.5 %multiply_subtract_fusion.2 = (f32[4,64,3,1280]{3,1,2,0:T(8,128)S(1)}, f32[4,64,3,1280]{3,1,2,0:T(8,128)}, f32[4,64,3,1280]{3,1,2,0:T(8,128)}) fusion(f32[4,64,3,1280]{3,1,2,0:T(8,128)} %bitcast.98, f32[4,64,3,1279]{3,1,2,0:T(8,128)} %get-tuple-element.38, f32[4,64,3,1279]{3,1,2,0:T(8,128)} %get-tuple-element.37, f32[4,64,3,1216]{3,1,2,0:T(8,128)} %get-tuple-element.40, ...), kind=kLoop, calls=%fused_computation.28 | loop fusion | flops 14745600 | bytes 33689600 | tf_op jit(solution)/shard_map/sub | solution.py:48
  48.9 3.5 %fusion.72 = (f32[1,64,3,1280]{3,1,2,0:T(8,128)S(1)}, f32[1,64,3,1280]{3,1,2,0:T(8,128)S(1)}) fusion(f32[4,64,3,1280]{3,1,2,0:T(8,128)} %get-tuple-element.22, f32[4,64,3,1280]{3,1,2,0:T(8,128)} %get-tuple-element.24, f32[4,64,3,1280]{3,1,2,0:T(8,128)S(1)} %get-tuple-element.21, f32[1,4,64,3,1280]{4,2,3,1,0:T(8,128)S(1)} %copy-done.3, ...), kind=kLoop, calls=%fused_computation.116 | loop fusion | flops 5898240 | bytes 11857920 | tf_op jit(solution)/shard_map/add | solution.py:67
  55.3 1.9 %collective-permute-start.3 = (f32[4,64,1,1280]{3,1,2,0:T(8,128)S(1)}, f32[4,64,1,1280]{3,1,2,0:T(8,128)S(1)}, u32[]{:S(2)}, u32[]{:S(2)}) collective-permute-start(f32[4,64,1,1280]{3,1,2,0:T(8,128)S(1)} %get-tuple-element.35), channel_id=1, source_target_pairs={{0,1},{1,2},{2,3},{3,4},{4,5},{5,6},{6,7},{7,8},{8,9},{9,10},{10,1... | collective-permute-start | bytes 3932168 | tf_op jit(solution)/shard_map/ppermute | solution.py:22
  57.2 2.6 %collective-permute-start.2 = (f32[4,64,1,1280]{3,1,2,0:T(8,128)S(1)}, f32[4,64,1,1280]{3,1,2,0:T(8,128)S(1)}, u32[]{:S(2)}, u32[]{:S(2)}) collective-permute-start(f32[4,64,1,1280]{3,1,2,0:T(8,128)S(1)} %get-tuple-element.36), channel_id=1, source_target_pairs={{1,0},{2,1},{3,2},{4,3},{5,4},{6,5},{7,6},{8,7},{9,8},{10,9},{11,1... | collective-permute-start | bytes 3932168 | tf_op jit(solution)/shard_map/ppermute | solution.py:25
  59.8 4.4 %fusion.94 = (f32[4,64,3,1279]{3,1,2,0:T(8,128)}, f32[4,64,3,1279]{3,1,2,0:T(8,128)}) fusion(f32[4,64,3,1280]{3,1,2,0:T(8,128)S(1)} %broadcast_multiply_fusion), kind=kLoop, calls=%fused_computation.171 | loop fusion | bytes 15716352 | tf_op jit(solution)/shard_map/slice | solution.py:33
  64.2 4.4 %fusion.95 = (f32[4,64,3,1216]{3,1,2,0:T(8,128)}, f32[4,64,3,1216]{3,1,2,0:T(8,128)}) fusion(f32[4,64,3,1280]{3,1,2,0:T(8,128)S(1)} %broadcast_multiply_fusion), kind=kLoop, calls=%fused_computation.172 | loop fusion | bytes 14942208 | tf_op jit(solution)/shard_map/slice | solution.py:33
  68.6 3.1 %collective-permute-done.3 = f32[4,64,1,1280]{3,1,2,0:T(8,128)S(1)} collective-permute-done((f32[4,64,1,1280]{3,1,2,0:T(8,128)S(1)}, f32[4,64,1,1280]{3,1,2,0:T(8,128)S(1)}, u32[]{:S(2)}, u32[]{:S(2)}) %collective-permute-start.3) | collective-permute-done | bytes 1310752 | tf_op jit(solution)/shard_map/ppermute | solution.py:22
  71.7 6.5 %collective-permute-done.2 = f32[4,64,1,1280]{3,1,2,0:T(8,128)S(1)} collective-permute-done((f32[4,64,1,1280]{3,1,2,0:T(8,128)S(1)}, f32[4,64,1,1280]{3,1,2,0:T(8,128)S(1)}, u32[]{:S(2)}, u32[]{:S(2)}) %collective-permute-start.2) | collective-permute-done | bytes 1310752 | tf_op jit(solution)/shard_map/ppermute | solution.py:25
  78.2 2.5 %subtract_multiply_fusion.2 = f32[4,64,3,1280]{3,1,2,0:T(8,128)} fusion(f32[4,64,1,1280]{3,1,2,0:T(8,128)S(1)} %collective-permute-done.2, f32[4,64,3,1280]{3,1,2,0:T(8,128)S(1)} %broadcast_multiply_fusion, f32[4,64,1,1280]{3,1,2,0:T(8,128)S(1)} %collective-permute-done.3), kind=kLoop, calls=%fused_computation.23 | loop fusion | flops 3932160 | bytes 10485760 | tf_op jit(solution)/shard_map/mul | solution.py:49
  80.7 9.3 %multiply_subtract_fusion.1 = (f32[4,64,3,1280]{3,1,2,0:T(8,128)}, f32[4,64,3,1280]{3,1,2,0:T(8,128)}) fusion(f32[4,64,3,1279]{3,1,2,0:T(8,128)} %get-tuple-element.32, f32[4,64,3,1279]{3,1,2,0:T(8,128)} %get-tuple-element.31, f32[4,64,3,1216]{3,1,2,0:T(8,128)} %get-tuple-element.34, f32[4,64,3,1216]{3,1,2,0:T(8,128)} %get-tuple-element.33, ...), kind=kLoop, calls=%fused_computation.25 | loop fusion | flops 17694720 | bytes 37621760 | tf_op jit(solution)/shard_map/sub | solution.py:48
  90.0 4.1 %fusion.48 = (f32[1,64,3,1280]{3,1,2,0:T(8,128)S(1)}, f32[1,64,3,1280]{3,1,2,0:T(8,128)S(1)}) fusion(f32[4,64,3,1280]{3,1,2,0:T(8,128)} %get-tuple-element.20, f32[4,64,3,1280]{3,1,2,0:T(8,128)} %subtract_multiply_fusion.2, f32[4,64,3,1280]{3,1,2,0:T(8,128)} %get-tuple-element.19, f32[4,64,3,1280]{3,1,2,0:T(8,128)S(1)} %broadcast_multiply_fusion, ...), kind=kLoop, calls=%fused_computation.84 | loop fusion | flops 5898240 | bytes 11857920 | tf_op jit(solution)/shard_map/add | solution.py:67
  95.1 1.1 copy-done.6
  97.2 1.1 fusion.1
  98.7 1.9 %collective-permute-start.5 = (f32[4,64,1,1280]{3,1,2,0:T(8,128)S(1)}, f32[4,64,1,1280]{3,1,2,0:T(8,128)S(1)}, u32[]{:S(2)}, u32[]{:S(2)}) collective-permute-start(f32[4,64,1,1280]{3,1,2,0:T(8,128)S(1)} %get-tuple-element.29), channel_id=1, source_target_pairs={{0,1},{1,2},{2,3},{3,4},{4,5},{5,6},{6,7},{7,8},{8,9},{9,10},{10,1... | collective-permute-start | bytes 3932168 | tf_op jit(solution)/shard_map/ppermute | solution.py:22
  100.6 2.6 %collective-permute-start.4 = (f32[4,64,1,1280]{3,1,2,0:T(8,128)S(1)}, f32[4,64,1,1280]{3,1,2,0:T(8,128)S(1)}, u32[]{:S(2)}, u32[]{:S(2)}) collective-permute-start(f32[4,64,1,1280]{3,1,2,0:T(8,128)S(1)} %get-tuple-element.30), channel_id=1, source_target_pairs={{1,0},{2,1},{3,2},{4,3},{5,4},{6,5},{7,6},{8,7},{9,8},{10,9},{11,1... | collective-permute-start | bytes 3932168 | tf_op jit(solution)/shard_map/ppermute | solution.py:25
  103.2 4.5 %fusion.92 = (f32[4,64,3,1216]{3,1,2,0:T(8,128)}, f32[4,64,3,1216]{3,1,2,0:T(8,128)}) fusion(f32[4,64,3,1280]{3,1,2,0:T(8,128)S(1)} %fusion.1), kind=kLoop, calls=%fused_computation.169 | loop fusion | bytes 14942208 | tf_op jit(solution)/shard_map/slice | solution.py:33
  107.7 4.5 %fusion.91 = (f32[4,64,3,1279]{3,1,2,0:T(8,128)}, f32[4,64,3,1279]{3,1,2,0:T(8,128)}) fusion(f32[4,64,3,1280]{3,1,2,0:T(8,128)S(1)} %fusion.1), kind=kLoop, calls=%fused_computation.168 | loop fusion | bytes 15716352 | tf_op jit(solution)/shard_map/slice | solution.py:33
  112.2 2.9 %collective-permute-done.5 = f32[4,64,1,1280]{3,1,2,0:T(8,128)S(1)} collective-permute-done((f32[4,64,1,1280]{3,1,2,0:T(8,128)S(1)}, f32[4,64,1,1280]{3,1,2,0:T(8,128)S(1)}, u32[]{:S(2)}, u32[]{:S(2)}) %collective-permute-start.5) | collective-permute-done | bytes 1310752 | tf_op jit(solution)/shard_map/ppermute | solution.py:22
  115.1 6.5 %collective-permute-done.4 = f32[4,64,1,1280]{3,1,2,0:T(8,128)S(1)} collective-permute-done((f32[4,64,1,1280]{3,1,2,0:T(8,128)S(1)}, f32[4,64,1,1280]{3,1,2,0:T(8,128)S(1)}, u32[]{:S(2)}, u32[]{:S(2)}) %collective-permute-start.4) | collective-permute-done | bytes 1310752 | tf_op jit(solution)/shard_map/ppermute | solution.py:25
  121.6 1.2 copy-done.17
  122.8 10.8 %multiply_subtract_fusion = (f32[4,64,3,1280]{3,1,2,0:T(8,128)}, f32[4,64,3,1280]{3,1,2,0:T(8,128)}, f32[4,64,3,1280]{3,1,2,0:T(8,128)}) fusion(f32[4,64,3,1280]{3,1,2,0:T(8,128)S(1)} %fusion.1, f32[4,64,3,1279]{3,1,2,0:T(8,128)} %get-tuple-element.26, f32[4,64,3,1279]{3,1,2,0:T(8,128)} %get-tuple-element.25, f32[4,64,3,1216]{3,1,2,0:T(8,128)} %get-tuple-element.28, ...), kind=kLoop, calls=%fused_computation.22 | loop fusion | flops 14745600 | bytes 33689600 | tf_op jit(solution)/shard_map/sub | solution.py:48
  133.6 4.1 %fusion.23 = (f32[1,1,64,3,1280]{4,2,3,1,0:T(8,128)S(1)}, f32[1,1,64,3,1280]{4,2,3,1,0:T(8,128)S(1)}) fusion(f32[4,64,3,1280]{3,1,2,0:T(8,128)} %get-tuple-element.18, f32[4,64,3,1280]{3,1,2,0:T(8,128)} %get-tuple-element.23, f32[4,64,3,1280]{3,1,2,0:T(8,128)} %get-tuple-element.17, f32[4,64,3,1280]{3,1,2,0:T(8,128)S(1)} %fusion.1, ...), kind=kLoop, calls=%fused_computation.51 | loop fusion | flops 5898240 | bytes 11857920 | tf_op jit(solution)/shard_map/stack | solution.py:90
  138.7 1.1 copy-done.9
  139.8 2.0 %fusion.30 = (f32[1,1,64,3,1280]{4,2,3,1,0:T(8,128)S(1)}, f32[1,1,64,3,1280]{4,2,3,1,0:T(8,128)}) fusion(f32[4,64,3,1280]{3,1,2,0:T(8,128)S(1)} %copy-done.9, f32[4,64,3,1280]{3,1,2,0:T(8,128)S(1)} %copy-done.8, f32[4,64,3,1280]{3,1,2,0:T(8,128)S(1)} %copy-done.7, f32[4,64,3,1280]{3,1,2,0:T(8,128)S(1)} %fusion.1, f32[3,1280]{1,0:T(4,128)S(1)} %get-tuple-element.49, ...), kind=kLoop, calls=%fused_computation.60 | loop fusion | flops 5898240 | bytes 11857920 | tf_op jit(solution)/shard_map/stack | solution.py:90
  141.8 4.5 %fusion.3 = f32[1,4,64,3,1280]{4,2,3,1,0:T(8,128)} fusion(f32[1,1,64,3,1280]{4,2,3,1,0:T(8,128)} %get-tuple-element.6, f32[1,1,64,3,1280]{4,2,3,1,0:T(8,128)S(1)} %get-tuple-element.8, f32[1,1,64,3,1280]{4,2,3,1,0:T(8,128)S(1)} %get-tuple-element.7, f32[1,1,64,3,1280]{4,2,3,1,0:T(8,128)S(1)} %get-tuple-element.5, f32[1,1,64,3,1280]{4,2,3,1,0:T(8,128)S(1)} %bitcast.108, ...), kind=kLoop, calls=%fused_computation.14 | loop fusion | flops 20643840 | bytes 19660800 | tf_op jit(solution)/shard_map/sub | solution.py:120
  (66 shorter events, 10.7 us)
Async XLA Ops:
  0.0 25.4 %copy-start = (s32[32]{0:T(128)S(1)}, s32[32]{0:T(128)}, u32[]{:S(2)}) copy-start(s32[32]{0:T(128)} %param.8) | copy-start | bytes 388
  1.7 25.9 %all-to-all-start = ((f32[8,4,3,4,256]{4,1,3,2,0:T(4,128)}), f32[8,4,3,4,256]{4,1,3,2,0:T(4,128)S(1)}, u32[]{:S(2)}, u32[]{:S(2)}) async-start(f32[8,4,3,4,256]{4,1,3,2,0:T(4,128)} %stack.60), calls=%async_computation | async-start | bytes 786432 | tf_op jit(solution)/shard_map/all_to_all | solution.py:104
  9.0 7.2 %copy-start.2 = (f32[1,4,64,3,1280]{4,2,3,1,0:T(8,128)S(1)}, f32[1,4,64,3,1280]{4,2,3,1,0:T(8,128)}, u32[]{:S(2)}) copy-start(f32[1,4,64,3,1280]{4,2,3,1,0:T(8,128)} %param.5) | copy-start | bytes 11796484
  11.1 17.7 %collective-permute-start.1 = (f32[4,64,1,1280]{3,1,2,0:T(8,128)S(1)}, f32[4,64,1,1280]{3,1,2,0:T(8,128)}, u32[]{:S(2)}, u32[]{:S(2)}) collective-permute-start(f32[4,64,1,1280]{3,1,2,0:T(8,128)S(1)} %get-tuple-element.41), channel_id=1, source_target_pairs={{0,1},{1,2},{2,3},{3,4},{4,5},{5,6},{6,7},{7,8},{8,9},{9,10},{10,1... | collective-permute-start | bytes 3932168 | tf_op jit(solution)/shard_map/ppermute | solution.py:22
  14.3 21.1 %collective-permute-start = (f32[4,64,1,1280]{3,1,2,0:T(8,128)S(1)}, f32[4,64,1,1280]{3,1,2,0:T(8,128)}, u32[]{:S(2)}, u32[]{:S(2)}) collective-permute-start(f32[4,64,1,1280]{3,1,2,0:T(8,128)S(1)} %get-tuple-element.42), channel_id=1, source_target_pairs={{1,0},{2,1},{3,2},{4,3},{5,4},{6,5},{7,6},{8,7},{9,8},{10,9},{11,1... | collective-permute-start | bytes 3932168 | tf_op jit(solution)/shard_map/ppermute | solution.py:25
  20.8 4.5 %copy-start.18 = (s32[8,6]{1,0:T(8,128)S(1)}, s32[8,6]{1,0:T(8,128)}, u32[]{:S(2)}) copy-start(s32[8,6]{1,0:T(8,128)} %param.7) | copy-start | bytes 580
  25.3 1.0 copy-start.19
  35.4 13.5 %copy-start.3 = (f32[1,4,64,3,1280]{4,2,3,1,0:T(8,128)S(1)}, f32[1,4,64,3,1280]{4,2,3,1,0:T(8,128)}, u32[]{:S(2)}) copy-start(f32[1,4,64,3,1280]{4,2,3,1,0:T(8,128)} %param.5) | copy-start | bytes 11796484
  48.9 3.5 %copy-start.10 = (f32[4,64,3,1280]{3,1,2,0:T(8,128)S(1)}, f32[4,64,3,1280]{3,1,2,0:T(8,128)}, u32[]{:S(2)}) copy-start(f32[4,64,3,1280]{3,1,2,0:T(8,128)} %get-tuple-element.22) | copy-start | bytes 11796484
  48.9 4.5 %copy-start.11 = (f32[4,64,3,1280]{3,1,2,0:T(8,128)S(1)}, f32[4,64,3,1280]{3,1,2,0:T(8,128)}, u32[]{:S(2)}) copy-start(f32[4,64,3,1280]{3,1,2,0:T(8,128)} %get-tuple-element.24) | copy-start | bytes 11796484
  55.3 16.5 %collective-permute-start.3 = (f32[4,64,1,1280]{3,1,2,0:T(8,128)S(1)}, f32[4,64,1,1280]{3,1,2,0:T(8,128)S(1)}, u32[]{:S(2)}, u32[]{:S(2)}) collective-permute-start(f32[4,64,1,1280]{3,1,2,0:T(8,128)S(1)} %get-tuple-element.35), channel_id=1, source_target_pairs={{0,1},{1,2},{2,3},{3,4},{4,5},{5,6},{6,7},{7,8},{8,9},{9,10},{10,1... | collective-permute-start | bytes 3932168 | tf_op jit(solution)/shard_map/ppermute | solution.py:22
  57.2 21.0 %collective-permute-start.2 = (f32[4,64,1,1280]{3,1,2,0:T(8,128)S(1)}, f32[4,64,1,1280]{3,1,2,0:T(8,128)S(1)}, u32[]{:S(2)}, u32[]{:S(2)}) collective-permute-start(f32[4,64,1,1280]{3,1,2,0:T(8,128)S(1)} %get-tuple-element.36), channel_id=1, source_target_pairs={{1,0},{2,1},{3,2},{4,3},{5,4},{6,5},{7,6},{8,7},{9,8},{10,9},{11,1... | collective-permute-start | bytes 3932168 | tf_op jit(solution)/shard_map/ppermute | solution.py:25
  90.0 4.1 %copy-start.4 = (f32[4,64,3,1280]{3,1,2,0:T(8,128)S(1)}, f32[4,64,3,1280]{3,1,2,0:T(8,128)}, u32[]{:S(2)}) copy-start(f32[4,64,3,1280]{3,1,2,0:T(8,128)} %subtract_multiply_fusion.2) | copy-start | bytes 11796484
  90.0 5.1 %copy-start.5 = (f32[4,64,3,1280]{3,1,2,0:T(8,128)S(1)}, f32[4,64,3,1280]{3,1,2,0:T(8,128)}, u32[]{:S(2)}) copy-start(f32[4,64,3,1280]{3,1,2,0:T(8,128)} %get-tuple-element.19) | copy-start | bytes 11796484
  90.0 6.2 %copy-start.6 = (f32[4,64,3,1280]{3,1,2,0:T(8,128)S(1)}, f32[4,64,3,1280]{3,1,2,0:T(8,128)}, u32[]{:S(2)}) copy-start(f32[4,64,3,1280]{3,1,2,0:T(8,128)} %get-tuple-element.20) | copy-start | bytes 11796484
  97.2 1.2 copy-start.12
  97.2 1.2 copy-start.14
  98.7 16.5 %collective-permute-start.5 = (f32[4,64,1,1280]{3,1,2,0:T(8,128)S(1)}, f32[4,64,1,1280]{3,1,2,0:T(8,128)S(1)}, u32[]{:S(2)}, u32[]{:S(2)}) collective-permute-start(f32[4,64,1,1280]{3,1,2,0:T(8,128)S(1)} %get-tuple-element.29), channel_id=1, source_target_pairs={{0,1},{1,2},{2,3},{3,4},{4,5},{5,6},{6,7},{7,8},{8,9},{9,10},{10,1... | collective-permute-start | bytes 3932168 | tf_op jit(solution)/shard_map/ppermute | solution.py:22
  100.6 21.0 %collective-permute-start.4 = (f32[4,64,1,1280]{3,1,2,0:T(8,128)S(1)}, f32[4,64,1,1280]{3,1,2,0:T(8,128)S(1)}, u32[]{:S(2)}, u32[]{:S(2)}) collective-permute-start(f32[4,64,1,1280]{3,1,2,0:T(8,128)S(1)} %get-tuple-element.30), channel_id=1, source_target_pairs={{1,0},{2,1},{3,2},{4,3},{5,4},{6,5},{7,6},{8,7},{9,8},{10,9},{11,1... | collective-permute-start | bytes 3932168 | tf_op jit(solution)/shard_map/ppermute | solution.py:25
  115.1 6.5 %copy-start.16 = (f32[4,64,1,1280]{3,1,2,0:T(8,128)}, f32[4,64,1,1280]{3,1,2,0:T(8,128)S(1)}, u32[]{:S(2)}) copy-start(f32[4,64,1,1280]{3,1,2,0:T(8,128)S(1)} %collective-permute-done.5) | copy-start | bytes 3932164
  121.6 1.2 copy-start.17
  133.6 4.1 %copy-start.7 = (f32[4,64,3,1280]{3,1,2,0:T(8,128)S(1)}, f32[4,64,3,1280]{3,1,2,0:T(8,128)}, u32[]{:S(2)}) copy-start(f32[4,64,3,1280]{3,1,2,0:T(8,128)} %get-tuple-element.17) | copy-start | bytes 11796484
  133.6 5.1 %copy-start.8 = (f32[4,64,3,1280]{3,1,2,0:T(8,128)S(1)}, f32[4,64,3,1280]{3,1,2,0:T(8,128)}, u32[]{:S(2)}) copy-start(f32[4,64,3,1280]{3,1,2,0:T(8,128)} %get-tuple-element.18) | copy-start | bytes 11796484
  133.6 6.2 %copy-start.9 = (f32[4,64,3,1280]{3,1,2,0:T(8,128)S(1)}, f32[4,64,3,1280]{3,1,2,0:T(8,128)}, u32[]{:S(2)}) copy-start(f32[4,64,3,1280]{3,1,2,0:T(8,128)} %get-tuple-element.23) | copy-start | bytes 11796484
  139.8 2.0 %copy-start.13 = (f32[1,64,3,1280]{3,1,2,0:T(8,128)S(1)}, f32[1,64,3,1280]{3,1,2,0:T(8,128)}, u32[]{:S(2)}) copy-start(f32[1,64,3,1280]{3,1,2,0:T(8,128)} %copy-done.12) | copy-start | bytes 2949124
  139.8 2.0 %copy-start.15 = (f32[1,64,3,1280]{3,1,2,0:T(8,128)S(1)}, f32[1,64,3,1280]{3,1,2,0:T(8,128)}, u32[]{:S(2)}) copy-start(f32[1,64,3,1280]{3,1,2,0:T(8,128)} %copy-done.14) | copy-start | bytes 2949124
  141.8 4.5 %copy-start.1 = (s32[32]{0:T(128)S(1)}, s32[32]{0:T(128)}, u32[]{:S(2)}) copy-start(s32[32]{0:T(128)} %param.8) | copy-start | bytes 388
